TPU v7x, 256 devices: a whole 4x4x8 slice. The times are simulated.
256 devices in a mesh: prow: 8 (over z_hi, core), pcol: 32 (over x, z_lo, y).
Axes of the slice: x: 4, y: 4, z: 8 (z_hi: 4, z_lo: 2; z = z_hi * 2 + z_lo), core: 2. Of those that a mesh axis runs over, the one named last changes fastest.
Arguments:
- slab: float32 [2048, 98304], P('pcol', 'prow'), may hold values from -6 to 6
- vectors: float32 [98304, 512], P(('prow', 'pcol')), may hold values from -0.01953125 to 0.01953125
- tfactors: float32 [4, 128, 128], replicated, as said below
Outputs:
- transformed: float32 [2048, 98304], P('pcol', 'prow')
Inputs may be any that keep to these rules, and one draw needn't show every extreme that they name: Each tfactors[k] is upper triangular with diagonal entries between 1 and 2.
All inputs are finite; a program needn't handle non-finite values.
Results may differ from a plain program's by a relative error of at most 0.0001.
Values sent between devices are 32-bit elements; how exact they have to be, the bound alone decides.
No kernel may reach another device: no remote copies, remote signals or barrier semaphores. Data moves between devices by JAX's collectives and lax.ppermute only.
A program may use at most 128 MiB of HBM per device.

v0:
```python
import jax
import jax.numpy as jnp
from jax import lax
from jax.sharding import PartitionSpec as P


def matmul(left, right):
    return jnp.dot(left, right, precision=lax.Precision.HIGHEST, preferred_element_type=jnp.float32)


def per_device(slab, vectors, tfactors):
    count = tfactors.shape[0]
    width = tfactors.shape[1]
    work = slab
    for k in reversed(range(count)):
        basis = lax.all_gather(vectors[:, k * width : (k + 1) * width], "pcol", axis=0, tiled=True)
        products = lax.psum(matmul(work, basis), "prow")
        work = work - matmul(matmul(products, tfactors[k].T), basis.T)
    return work


def solution(mesh):
    in_specs = (P("pcol", "prow"), P(("prow", "pcol"), None), P())
    out_specs = P("pcol", "prow")
    return jax.shard_map(
        per_device, mesh=mesh, in_specs=in_specs, out_specs=out_specs, check_vma=False
    )
```

profile of v0, /device:TPU:8, one launch (start us, length us, event | category | flops | bytes accessed | tf_op | source)
XLA Modules:
  0.0 729.5 jit_solution(4784247094145726816)
XLA Ops:
  6.5 0.0 all-gather.5.cloned.1.call-start
  6.5 2.1 fusion.12
  8.6 0.0 all-gather.5.cloned.1.call-update
  8.7 0.0 all-gather.7.cloned.1.call-start
  8.7 0.7 all-gather.7.cloned.1.call-update
  9.4 0.0 all-gather.9.cloned.1.call-start
  9.5 0.7 all-gather.9.cloned.1.call-update
  10.2 0.0 all-gather.11.cloned.1.call-start
  10.2 0.5 all-gather.11.cloned.1.call-update
  10.7 0.0 copy-start.2
  10.7 166.6 %all-gather.5.cloned.1.call-done = f32[12288,128]{1,0:T(8,128)} async-done(((f32[384,128]{1,0:T(8,128)}), f32[12288,128]{1,0:T(8,128)}) %all-gather.5.cloned.1.call-update) | async-done | bytes 6291472 | tf_op jit(solution)/shard_map/all_gather | solution.py:16
  177.3 6.4 fusion.13
  183.8 27.2 %psum.28 = f32[64,128]{1,0:T(8,128)S(1)} all-reduce(f32[64,128]{1,0:T(8,128)S(1)} %fusion.13), channel_id=1, replica_groups=mesh['prow'=8,'pcol'=32] {'prow'}, use_global_device_ids=true, to_apply=%region_0.0 | all-reduce | flops 8192 | bytes 65536 | tf_op jit(solution)/shard_map/psum | solution.py:17
  211.0 0.2 fusion.6
  211.2 9.4 %convolution_subtract_fusion.3 = f32[64,12288]{1,0:T(8,128)S(1)} fusion(f32[64,12288]{1,0:T(8,128)} %param.3, f32[64,128]{1,0:T(8,128)S(1)} %fusion.6, f32[12288,128]{1,0:T(8,128)} %all-gather.5.cloned.1.call-done), kind=kOutput, calls=%fused_computation.3 | convolution fusion | flops 1208745984 | bytes 12615680 | tf_op jit(solution)/shard_map/dot_general | solution.py:8
  220.6 0.0 copy-start.1
  220.6 124.5 %all-gather.7.cloned.1.call-done = f32[12288,128]{1,0:T(8,128)} async-done(((f32[384,128]{1,0:T(8,128)}), f32[12288,128]{1,0:T(8,128)}) %all-gather.7.cloned.1.call-update) | async-done | bytes 6291472 | tf_op jit(solution)/shard_map/all_gather | solution.py:16
  345.1 5.9 fusion.14
  351.1 0.0 copy-done.1
  351.1 27.4 %psum.29 = f32[64,128]{1,0:T(8,128)S(1)} all-reduce(f32[64,128]{1,0:T(8,128)S(1)} %fusion.14), channel_id=1, replica_groups=mesh['prow'=8,'pcol'=32] {'prow'}, use_global_device_ids=true, to_apply=%region_1.0 | all-reduce | flops 8192 | bytes 65536 | tf_op jit(solution)/shard_map/psum | solution.py:17
  378.4 0.2 fusion.4
  378.7 9.4 %convolution_subtract_fusion.2 = f32[64,12288]{1,0:T(8,128)S(1)} fusion(f32[64,12288]{1,0:T(8,128)} %copy-done.1, f32[64,128]{1,0:T(8,128)S(1)} %fusion.4, f32[12288,128]{1,0:T(8,128)} %all-gather.7.cloned.1.call-done), kind=kOutput, calls=%fused_computation.2 | convolution fusion | flops 1208745984 | bytes 12615680 | tf_op jit(solution)/shard_map/dot_general | solution.py:8
  388.1 123.8 %all-gather.9.cloned.1.call-done = f32[12288,128]{1,0:T(8,128)} async-done(((f32[384,128]{1,0:T(8,128)}), f32[12288,128]{1,0:T(8,128)}) %all-gather.9.cloned.1.call-update) | async-done | bytes 6291472 | tf_op jit(solution)/shard_map/all_gather | solution.py:16
  511.9 5.9 fusion.15
  517.8 27.2 %psum.30 = f32[64,128]{1,0:T(8,128)S(1)} all-reduce(f32[64,128]{1,0:T(8,128)S(1)} %fusion.15), channel_id=1, replica_groups=mesh['prow'=8,'pcol'=32] {'prow'}, use_global_device_ids=true, to_apply=%region_2.0 | all-reduce | flops 8192 | bytes 65536 | tf_op jit(solution)/shard_map/psum | solution.py:17
  545.0 0.2 fusion.2
  545.3 10.1 %convolution_subtract_fusion.1 = f32[64,12288]{1,0:T(8,128)} fusion(f32[64,12288]{1,0:T(8,128)S(1)} %convolution_subtract_fusion.2, f32[64,128]{1,0:T(8,128)S(1)} %fusion.2, f32[12288,128]{1,0:T(8,128)} %all-gather.9.cloned.1.call-done), kind=kOutput, calls=%fused_computation.1 | convolution fusion | flops 1208745984 | bytes 12615680 | tf_op jit(solution)/shard_map/dot_general | solution.py:8
  555.3 123.4 %all-gather.11.cloned.1.call-done = f32[12288,128]{1,0:T(8,128)} async-done(((f32[384,128]{1,0:T(8,128)}), f32[12288,128]{1,0:T(8,128)}) %all-gather.11.cloned.1.call-update) | async-done | bytes 6291472 | tf_op jit(solution)/shard_map/all_gather | solution.py:16
  678.7 6.4 fusion.16
  685.1 27.5 %psum.31 = f32[64,128]{1,0:T(8,128)S(1)} all-reduce(f32[64,128]{1,0:T(8,128)S(1)} %fusion.16), channel_id=1, replica_groups=mesh['prow'=8,'pcol'=32] {'prow'}, use_global_device_ids=true, to_apply=%region_3.0 | all-reduce | flops 8192 | bytes 65536 | tf_op jit(solution)/shard_map/psum | solution.py:17
  712.6 0.2 fusion
  712.9 10.1 %convolution_subtract_fusion = f32[64,12288]{1,0:T(8,128)} fusion(f32[64,12288]{1,0:T(8,128)S(1)} %copy-done, f32[64,128]{1,0:T(8,128)S(1)} %fusion, f32[12288,128]{1,0:T(8,128)} %all-gather.11.cloned.1.call-done), kind=kOutput, calls=%fused_computation | convolution fusion | flops 1208745984 | bytes 12615680 | tf_op jit(solution)/shard_map/dot_general | solution.py:8
  (3 shorter events, 0.0 us)
Async XLA Ops:
  6.5 170.8 %all-gather.5.cloned.1.call-start = ((), (), s32[]{:S(2)}) async-start(), calls=%async_computation | async-start | bytes 6488064 | tf_op jit(solution)/shard_map/all_gather | solution.py:16
  8.7 336.4 %all-gather.7.cloned.1.call-start = ((), (), s32[]{:S(2)}) async-start(), calls=%async_computation.1 | async-start | bytes 6488064 | tf_op jit(solution)/shard_map/all_gather | solution.py:16
  9.4 502.5 %all-gather.9.cloned.1.call-start = ((), (), s32[]{:S(2)}) async-start(), calls=%async_computation.2 | async-start | bytes 6488064 | tf_op jit(solution)/shard_map/all_gather | solution.py:16
  10.2 668.5 %all-gather.11.cloned.1.call-start = ((), (), s32[]{:S(2)}) async-start(), calls=%async_computation.3 | async-start | bytes 6488064 | tf_op jit(solution)/shard_map/all_gather | solution.py:16
  10.7 200.2 %copy-start.2 = (f32[4,128,128]{2,1,0:T(8,128)S(1)}, f32[4,128,128]{2,1,0:T(8,128)}, u32[]{:S(2)}) copy-start(f32[4,128,128]{2,1,0:T(8,128)} %param.5) | copy-start | bytes 786436
  220.6 130.4 %copy-start.1 = (f32[64,12288]{1,0:T(8,128)}, f32[64,12288]{1,0:T(8,128)S(1)}, u32[]{:S(2)}) copy-start(f32[64,12288]{1,0:T(8,128)S(1)} %convolution_subtract_fusion.3) | copy-start | bytes 9437188
  555.3 157.5 %copy-start = (f32[64,12288]{1,0:T(8,128)S(1)}, f32[64,12288]{1,0:T(8,128)}, u32[]{:S(2)}) copy-start(f32[64,12288]{1,0:T(8,128)} %convolution_subtract_fusion.1) | copy-start | bytes 9437188
Sparse Core Ops, SparseCore 0:
  9.1 168.1 all-gather.4
  179.1 165.9 all-gather.6
  346.9 164.9 all-gather.8
  513.5 165.1 all-gather.10
where the time goes:
time: 730 us; the launch traced here: 729 us
  waiting for transfers between devices  540 us (74%)
  blocking collectives  109 us (15%)
  matrix products  64.6 us (9%)
  between operations  13.2 us (2%)
    all_gather x4, waiting for transfers between devices, per_device(): lax.all_gather(vectors[:, k * width:(k + 1) * width], 'pcol', axis=0, til...  538 us
    psum x4, blocking collectives, per_device(): products = lax.psum(matmul(work, basis), 'prow')  109 us
    dot_general x12, matrix products, matmul(): jnp.dot(left, right, precision=lax.Precision.HIGHEST, preferred_element_t...  64.6 us
  transfers between devices with their start and end apart: 4, of which 4 were waited for; matrix products, arithmetic and copies ran while one was open for 7% of the time, Pallas kernels for 0%

commit v1 on v0

--- a/solution.py
+++ b/solution.py
@@ -13,7 +13,9 @@
     width = tfactors.shape[1]
     work = slab
     for k in reversed(range(count)):
-        basis = lax.all_gather(vectors[:, k * width : (k + 1) * width], "pcol", axis=0, tiled=True)
+        x = vectors[:, k * width : (k + 1) * width]
+        sent = jnp.stack([x] * lax.axis_size("pcol"))
+        basis = jnp.concatenate(lax.all_to_all(sent, "pcol", 0, 0), axis=0)
         products = lax.psum(matmul(work, basis), "prow")
         work = work - matmul(matmul(products, tfactors[k].T), basis.T)
     return work

time: 730 us -> 510 us (0.70)
  the two profiles are of different devices: /device:TPU:8 before, /device:TPU:46 now
where the time goes in v1:
time: 510 us
  blocking collectives  429 us (84%)
  matrix products  61 us (12%)
  local copies, waits for them, and re-layouts  10.1 us (2%)
  starting transfers between devices  9.54 us (2%)
    all_to_all x3, blocking collectives, per_device(): basis = jnp.concatenate(lax.all_to_all(sent, 'pcol', 0, 0), axis=0)  234 us
    psum x4, blocking collectives, per_device(): products = lax.psum(matmul(work, basis), 'prow')  195 us
    dot_general x12, matrix products, matmul(): jnp.dot(left, right, precision=lax.Precision.HIGHEST, preferred_element_t...  61 us
  transfers between devices with their start and end apart: 1, of which 0 were waited for; matrix products, arithmetic and copies ran while one was open for 9% of the time, Pallas kernels for 0%

profile of v1, /device:TPU:46, one launch (start us, length us, event | category | flops | bytes accessed | tf_op | source)
XLA Modules:
  0.0 509.7 jit_solution(17300750147810188171)
XLA Ops:
  0.0 1.3 fusion.12
  1.3 0.7 stack.8
  2.0 78.6 %all_to_all.20 = f32[32,384,128]{2,1,0:T(8,128)} all-to-all(f32[32,384,128]{2,1,0:T(8,128)S(1)} %stack.8), channel_id=1, replica_groups=mesh['prow'=8,'pcol'=32] {'pcol'}, dimensions={0} | all-to-all | bytes 12582912 | tf_op jit(solution)/shard_map/all_to_all | solution.py:18
  80.6 0.7 stack.9
  81.3 79.7 %all_to_all.21 = f32[32,384,128]{2,1,0:T(8,128)} all-to-all(f32[32,384,128]{2,1,0:T(8,128)S(1)} %stack.9), channel_id=1, replica_groups=mesh['prow'=8,'pcol'=32] {'pcol'}, dimensions={0} | all-to-all | bytes 12582912 | tf_op jit(solution)/shard_map/all_to_all | solution.py:18
  160.9 0.7 stack.10
  161.6 76.1 %all_to_all.22 = f32[32,384,128]{2,1,0:T(8,128)} all-to-all(f32[32,384,128]{2,1,0:T(8,128)S(1)} %stack.10), channel_id=1, replica_groups=mesh['prow'=8,'pcol'=32] {'pcol'}, dimensions={0} | all-to-all | bytes 12582912 | tf_op jit(solution)/shard_map/all_to_all | solution.py:18
  237.7 3.4 stack.11
  241.1 9.5 %all-to-all-start.3 = ((f32[32,384,128]{2,1,0:T(8,128)}), f32[32,384,128]{2,1,0:T(8,128)}, u32[]{:S(2)}, u32[]{:S(2)}) async-start(f32[32,384,128]{2,1,0:T(8,128)} %stack.11), calls=%async_computation.3 | async-start | bytes 12582912 | tf_op jit(solution)/shard_map/all_to_all | solution.py:18
  250.7 0.0 copy-start.3
  250.7 6.0 %fusion.13 = f32[64,128]{1,0:T(8,128)S(1)} fusion(f32[64,12288]{1,0:T(8,128)S(1)} %copy-done.2, f32[12288,128]{1,0:T(8,128)} %bitcast.42), kind=kOutput, calls=%fused_computation.17 | convolution fusion | flops 1207959552 | bytes 9469952 | tf_op jit(solution)/shard_map/dot_general | solution.py:8
  256.7 112.4 %psum.28 = f32[64,128]{1,0:T(8,128)S(1)} all-reduce(f32[64,128]{1,0:T(8,128)S(1)} %fusion.13), channel_id=1, replica_groups=mesh['prow'=8,'pcol'=32] {'prow'}, use_global_device_ids=true, to_apply=%region_0.0 | all-reduce | flops 8192 | bytes 65536 | tf_op jit(solution)/shard_map/psum | solution.py:19
  369.1 0.2 fusion.6
  369.3 8.9 %convolution_subtract_fusion.3 = f32[64,12288]{1,0:T(8,128)S(1)} fusion(f32[64,12288]{1,0:T(8,128)S(1)} %copy-done.2, f32[64,128]{1,0:T(8,128)S(1)} %fusion.6, f32[12288,128]{1,0:T(8,128)} %bitcast.43), kind=kOutput, calls=%fused_computation.3 | convolution fusion | flops 1208745984 | bytes 12615680 | tf_op jit(solution)/shard_map/dot_general | solution.py:8
  378.3 0.0 copy-start.1
  378.3 1.7 copy-done.1
  379.9 6.1 %fusion.14 = f32[64,128]{1,0:T(8,128)S(1)} fusion(f32[64,12288]{1,0:T(8,128)S(1)} %convolution_subtract_fusion.3, f32[12288,128]{1,0:T(8,128)} %bitcast.40), kind=kOutput, calls=%fused_computation.18 | convolution fusion | flops 1207959552 | bytes 9469952 | tf_op jit(solution)/shard_map/dot_general | solution.py:8
  386.1 27.4 %psum.29 = f32[64,128]{1,0:T(8,128)S(1)} all-reduce(f32[64,128]{1,0:T(8,128)S(1)} %fusion.14), channel_id=1, replica_groups=mesh['prow'=8,'pcol'=32] {'prow'}, use_global_device_ids=true, to_apply=%region_1.0 | all-reduce | flops 8192 | bytes 65536 | tf_op jit(solution)/shard_map/psum | solution.py:19
  413.5 0.2 fusion.4
  413.7 0.0 slice-start.1
  413.7 9.6 %convolution_subtract_fusion.2 = f32[64,12288]{1,0:T(8,128)S(1)} fusion(f32[64,12288]{1,0:T(8,128)} %copy-done.1, f32[64,128]{1,0:T(8,128)S(1)} %fusion.4, f32[12288,128]{1,0:T(8,128)} %bitcast.41), kind=kOutput, calls=%fused_computation.2 | convolution fusion | flops 1208745984 | bytes 12615680 | tf_op jit(solution)/shard_map/dot_general | solution.py:8
  423.3 0.0 copy-start
  423.3 1.7 copy-done
  425.0 4.0 fusion.15
  429.0 27.5 %psum.30 = f32[64,128]{1,0:T(8,128)S(1)} all-reduce(f32[64,128]{1,0:T(8,128)S(1)} %fusion.15), channel_id=1, replica_groups=mesh['prow'=8,'pcol'=32] {'prow'}, use_global_device_ids=true, to_apply=%region_2.0 | all-reduce | flops 8192 | bytes 65536 | tf_op jit(solution)/shard_map/psum | solution.py:19
  456.5 0.2 fusion.2
  456.7 9.4 %convolution_subtract_fusion.1 = f32[64,12288]{1,0:T(8,128)S(1)} fusion(f32[64,12288]{1,0:T(8,128)} %copy-done, f32[64,128]{1,0:T(8,128)S(1)} %fusion.2, f32[12288,128]{1,0:T(8,128)} %bitcast.36), kind=kOutput, calls=%fused_computation.1 | convolution fusion | flops 1208745984 | bytes 12615680 | tf_op jit(solution)/shard_map/dot_general | solution.py:8
  466.1 0.0 all-to-all-done.3
  466.2 5.9 %fusion.16 = f32[64,128]{1,0:T(8,128)S(1)} fusion(f32[64,12288]{1,0:T(8,128)S(1)} %convolution_subtract_fusion.1, f32[12288,128]{1,0:T(8,128)} %bitcast.6), kind=kOutput, calls=%fused_computation.20 | convolution fusion | flops 1207959552 | bytes 9469952 | tf_op jit(solution)/shard_map/dot_general | solution.py:8
  472.1 27.3 %psum.31 = f32[64,128]{1,0:T(8,128)S(1)} all-reduce(f32[64,128]{1,0:T(8,128)S(1)} %fusion.16), channel_id=1, replica_groups=mesh['prow'=8,'pcol'=32] {'prow'}, use_global_device_ids=true, to_apply=%region_3.0 | all-reduce | flops 8192 | bytes 65536 | tf_op jit(solution)/shard_map/psum | solution.py:19
  499.4 0.2 fusion
  499.7 10.1 %convolution_subtract_fusion = f32[64,12288]{1,0:T(8,128)} fusion(f32[64,12288]{1,0:T(8,128)S(1)} %convolution_subtract_fusion.1, f32[64,128]{1,0:T(8,128)S(1)} %fusion, f32[12288,128]{1,0:T(8,128)} %bitcast.6), kind=kOutput, calls=%fused_computation | convolution fusion | flops 1208745984 | bytes 12615680 | tf_op jit(solution)/shard_map/dot_general | solution.py:8
  (7 shorter events, 0.0 us)
Async XLA Ops:
  241.1 9.6 %copy-start.2 = (f32[64,12288]{1,0:T(8,128)S(1)}, f32[64,12288]{1,0:T(8,128)}, u32[]{:S(2)}) copy-start(f32[64,12288]{1,0:T(8,128)} %param.3) | copy-start | bytes 9437188
  241.1 225.0 %all-to-all-start.3 = ((f32[32,384,128]{2,1,0:T(8,128)}), f32[32,384,128]{2,1,0:T(8,128)}, u32[]{:S(2)}, u32[]{:S(2)}) async-start(f32[32,384,128]{2,1,0:T(8,128)} %stack.11), calls=%async_computation.3 | async-start | bytes 12582912 | tf_op jit(solution)/shard_map/all_to_all | solution.py:18
  250.7 118.4 %copy-start.3 = (f32[4,128,128]{2,1,0:T(8,128)S(1)}, f32[4,128,128]{2,1,0:T(8,128)}, u32[]{:S(2)}) copy-start(f32[4,128,128]{2,1,0:T(8,128)} %param.5) | copy-start | bytes 786436
  378.3 1.7 copy-start.1
  379.9 45.0 %slice-start = ((s8[6291456]{0:T(1024)(128)(4,1)}), s8[2097152]{0:T(1024)(128)(4,1)S(1)}, s32[]{:S(2)}) async-start(s8[6291456]{0:T(1024)(128)(4,1)} %bitcast.37), calls=%async_computation.4 | async-start | bytes 4194304
  413.7 11.3 %slice-start.1 = ((s8[6291456]{0:T(1024)(128)(4,1)}), s8[4194304]{0:T(1024)(128)(4,1)S(1)}, s32[]{:S(2)}) async-start(s8[6291456]{0:T(1024)(128)(4,1)} %bitcast.37), calls=%async_computation.5 | async-start | bytes 8388608
  423.3 1.7 copy-start
